TPU v7x, 512 devices: a whole 4x4x16 slice. The times are simulated.
512 devices in a mesh: row: 64 (over z_lo, x, core), col: 8 (over y, z_hi).
Axes of the slice: x: 4, y: 4, z: 16 (z_hi: 2, z_lo: 8; z = z_hi * 8 + z_lo), core: 2. Of those that a mesh axis runs over, the one named last changes fastest.
Arguments:
- u3: bfloat16 [2048, 64, 512], P(('row', 'col')), may hold values from -6 to 6
- g3: bfloat16 [2048, 64, 512], P(('row', 'col')), may hold values from -6 to 6
- ln3_w: float32 [512], replicated, may hold values from 0.25 to 1.75
- ln3_b: float32 [512], replicated, may hold values from -3 to 3
- bias3: float32 [2048], replicated, may hold values from -3 to 3
- gamma3: float32 [512], replicated, may hold values from 0.3 to 1.5
- kernel3: float32 [7, 7, 512], replicated, may hold values from -0.875 to 0.875
- expand3: bfloat16 [512, 2048], P(None, 'row'), may hold values from -0.25 to 0.25
- project3: bfloat16 [512, 2048], P(None, 'row'), may hold values from -0.125 to 0.125
- down_w: bfloat16 [1024, 512], P(None, 'row'), may hold values from -0.1875 to 0.1875
- dln_w: float32 [256], replicated, may hold values from 0.25 to 1.75
- y2: bfloat16 [4096, 128, 256], P('row', 'col'), may hold values from -6 to 6
- u2: bfloat16 [4096, 128, 256], P('row', 'col'), may hold values from -6 to 6
- ln2_w: float32 [256], replicated, may hold values from 0.25 to 1.75
- ln2_b: float32 [256], replicated, may hold values from -3 to 3
- bias2: float32 [1024], replicated, may hold values from -3 to 3
- gamma2: float32 [256], replicated, may hold values from 0.3 to 1.5
- kernel2: float32 [7, 7, 256], replicated, may hold values from -0.875 to 0.875
- expand2: bfloat16 [256, 1024], P(None, 'row'), may hold values from -0.375 to 0.375
- project2: bfloat16 [256, 1024], P(None, 'row'), may hold values from -0.1875 to 0.1875
- tissue: int32 [256, 8], P('row', 'col'), may hold values 0 or 1
Outputs:
- gx2: bfloat16 [4096, 128, 256], P('row', 'col')
Inputs may be any that keep to these rules, and one draw needn't show every extreme that they name: tissue marks tiles holding tissue.
All inputs are finite; a program needn't handle non-finite values. No bound on the sum of `tissue` on one device may be relied on, other than what follows from the above.
Results may differ from a plain program's by a relative error of at most 0.014.
Values may be sent and summed in bfloat16 or wider, within the bound.
No kernel may reach another device: no remote copies, remote signals or barrier semaphores. Data moves between devices by JAX's collectives and lax.ppermute only.
A program may use at most 64 MiB of HBM per device.

v0:
```python
import jax
import jax.numpy as jnp
from jax import lax
from jax.sharding import PartitionSpec as P

TILE = 16
EPS = 1e-06
ROOT_HALF = 0.7071067811865476
DENS = 0.3989422804014327


def padded_2(block, sides, width):
    for axis, dim in sides:
        count = lax.axis_size(axis)
        forward = [(i, i + 1) for i in range(count - 1)]
        backward = [(target, source) for source, target in forward]
        low = lax.ppermute(
            lax.slice_in_dim(block, block.shape[dim] - width, None, axis=dim), axis, forward
        )
        high = lax.ppermute(lax.slice_in_dim(block, 0, width, axis=dim), axis, backward)
        block = jnp.concatenate([low, block, high], axis=dim)
    return block


def block_grad(u, g, layernorm_weight, layernorm_bias, bias, gamma, expand, project):
    count = u.shape[0]
    width = u.shape[1]
    blk = min(count, 512)

    def one(pair):
        ub, gb = pair
        uf = ub.astype(jnp.float32)
        centered_input = uf - jnp.mean(uf, axis=-1, keepdims=True)
        inverse_deviation = lax.rsqrt(
            jnp.mean(centered_input * centered_input, axis=-1, keepdims=True) + EPS
        )
        standardized_input = centered_input * inverse_deviation
        normalized_output = (standardized_input * layernorm_weight + layernorm_bias).astype(
            jnp.bfloat16
        )
        hidden = jnp.dot(normalized_output, expand, preferred_element_type=jnp.float32) + bias
        scaled = (gamma * gb.astype(jnp.float32)).astype(jnp.bfloat16)
        grad_act = jnp.dot(scaled, project, preferred_element_type=jnp.float32)
        slope = 0.5 * (1.0 + jax.scipy.special.erf(hidden * ROOT_HALF)) + hidden * DENS * jnp.exp(
            -0.5 * hidden * hidden
        )
        grad_hid = (grad_act * slope).astype(jnp.bfloat16)
        grad_norm = lax.dot_general(
            grad_hid, expand, (((1,), (1,)), ((), ())), preferred_element_type=jnp.float32
        )
        projection_term = grad_norm * layernorm_weight
        upstream_gradient = inverse_deviation * (
            projection_term
            - jnp.mean(projection_term, axis=-1, keepdims=True)
            - standardized_input
            * jnp.mean(projection_term * standardized_input, axis=-1, keepdims=True)
        )
        return upstream_gradient.astype(jnp.bfloat16)

    result = lax.map(
        one, (u.reshape(count // blk, blk, width), g.reshape(count // blk, blk, width))
    )
    return result.reshape(count, width)


def spread(padded, kernel, height, width):
    total = jnp.zeros((height, width, padded.shape[2]), jnp.float32)
    for dy in range(7):
        for dx in range(7):
            total = total + kernel[dy, dx] * padded[
                6 - dy : 6 - dy + height, 6 - dx : 6 - dx + width
            ].astype(jnp.float32)
    return total


def norm_back(value, grad, gain):
    vf = value.astype(jnp.float32)
    centered_input = vf - jnp.mean(vf, axis=-1, keepdims=True)
    inverse_deviation = lax.rsqrt(
        jnp.mean(centered_input * centered_input, axis=-1, keepdims=True) + EPS
    )
    yhat = centered_input * inverse_deviation
    projection_term = grad * gain
    return inverse_deviation * (
        projection_term
        - jnp.mean(projection_term, axis=-1, keepdims=True)
        - yhat * jnp.mean(projection_term * yhat, axis=-1, keepdims=True)
    )


def project_down(grads, down_whole):
    return lax.dot_general(
        grads, down_whole, (((1,), (1,)), ((), ())), preferred_element_type=jnp.float32
    )


def on_device(
    u3,
    g3,
    ln3_w,
    ln3_b,
    bias3,
    gamma3,
    kernel3,
    expand3,
    project3,
    down_w,
    dln_w,
    y2,
    u2,
    ln2_w,
    ln2_b,
    bias2,
    gamma2,
    kernel2,
    expand2,
    project2,
    tissue,
):
    expand3, project3, down_w, expand2, project2 = (
        lax.all_gather(expand3, "row", axis=1, tiled=True),
        lax.all_gather(project3, "row", axis=1, tiled=True),
        lax.all_gather(down_w, "row", axis=1, tiled=True),
        lax.all_gather(expand2, "row", axis=1, tiled=True),
        lax.all_gather(project2, "row", axis=1, tiled=True),
    )
    rows3, width3, chans3 = u3.shape
    rows2, cols2, chans2 = y2.shape
    grad_u3 = block_grad(
        u3.reshape(-1, chans3),
        g3.reshape(-1, chans3),
        ln3_w,
        ln3_b,
        bias3,
        gamma3,
        expand3,
        project3,
    ).reshape(u3.shape)
    rimmed3 = padded_2(grad_u3, ((("row", "col"), 0),), 3)
    padded3 = jnp.pad(rimmed3, ((0, 0), (3, 3), (0, 0)))
    gx3 = (g3.astype(jnp.float32) + spread(padded3, kernel3, rows3, width3)).astype(jnp.bfloat16)
    grad_m = project_down(gx3.reshape(-1, chans3), down_w).astype(jnp.bfloat16)
    grad_m = grad_m.reshape(rows3, width3, 4 * chans2)
    moved = lax.all_to_all(grad_m, "col", split_axis=1, concat_axis=0, tiled=True)
    grad_mf = moved.astype(jnp.float32)
    grad_mf = (
        grad_mf.reshape(rows2 // 2, cols2 // 2, 2, 2, chans2)
        .transpose(0, 2, 1, 3, 4)
        .reshape(rows2, cols2, chans2)
    )
    grad_y = norm_back(y2, grad_mf, dln_w)
    tile_rows, tile_cols = tissue.shape
    pixel_mask = jnp.broadcast_to(
        tissue.astype(jnp.float32)[:, None, :, None], (tile_rows, TILE, tile_cols, TILE)
    ).reshape(rows2, cols2)
    g2 = (grad_y * pixel_mask[:, :, None]).astype(jnp.bfloat16)
    grad_u2 = block_grad(
        u2.reshape(-1, chans2),
        g2.reshape(-1, chans2),
        ln2_w,
        ln2_b,
        bias2,
        gamma2,
        expand2,
        project2,
    ).reshape(u2.shape)
    padded2 = padded_2(grad_u2, (("row", 0), ("col", 1)), 3)
    return (g2.astype(jnp.float32) + spread(padded2, kernel2, rows2, cols2)).astype(jnp.bfloat16)


def solution(mesh):
    placed = (
        P(("row", "col"), None, None),
        P(("row", "col"), None, None),
        P(),
        P(),
        P(),
        P(),
        P(),
        P(None, "row"),
        P(None, "row"),
        P(None, "row"),
        P(),
        P("row", "col", None),
        P("row", "col", None),
        P(),
        P(),
        P(),
        P(),
        P(),
        P(None, "row"),
        P(None, "row"),
        P("row", "col"),
    )
    return jax.shard_map(
        on_device, mesh=mesh, in_specs=placed, out_specs=P("row", "col", None), check_vma=False
    )
```

profile of v0, /device:TPU:10, one launch (start us, length us, event | category | flops | bytes accessed | tf_op | source)
XLA Modules:
  0.0 729.9 jit_solution(1171352033100653243)
XLA Ops:
  6.5 0.7 all-gather.6.cloned.1.call-update
  7.3 0.7 all-gather.4.cloned.1.call-update
  8.1 0.7 all-gather.8.cloned.1.call-update
  8.7 1.1 convert_reduce_fusion.2
  9.8 1.2 multiply_reduce_fusion.2
  11.1 1.1 fusion.96
  12.1 1.2 fusion.95
  13.4 1.0 fusion.79
  14.4 1.2 add_convert_fusion.2
  15.6 118.1 %all-gather.6.cloned.1.call-done = bf16[512,2048]{0,1:T(8,128)(2,1)} async-done(((bf16[512,32]{0,1:T(8,128)(2,1)}), bf16[512,2048]{0,1:T(8,128)(2,1)}) %all-gather.6.cloned.1.call-update) | async-done | bytes 2097168 | tf_op jit(solution)/shard_map/all_gather | solution.py:121
  133.7 3.8 convolution_add_fusion
  137.6 114.7 %all-gather.4.cloned.1.call-done = bf16[512,2048]{0,1:T(8,128)(2,1)} async-done(((bf16[512,32]{0,1:T(8,128)(2,1)}), bf16[512,2048]{0,1:T(8,128)(2,1)}) %all-gather.4.cloned.1.call-update) | async-done | bytes 2097168 | tf_op jit(solution)/shard_map/all_gather | solution.py:122
  252.3 4.1 fusion.90
  256.4 0.2 multiply_convert_fusion
  256.7 8.3 %collective-permute-start = (bf16[3,64,512]{2,1,0:T(8,128)(2,1)S(1)}, bf16[3,64,512]{2,1,0:T(8,128)(2,1)S(1)}, u32[]{:S(2)}, u32[]{:S(2)}) collective-permute-start(bf16[3,64,512]{2,1,0:T(8,128)(2,1)S(1)} %bitcast.212), channel_id=1, source_target_pairs={{0,1},{1,2},{2,3},{3,4},{4,5},{5,6},{6,7},{7,8},{8,9},{9,10},{10,1... | collective-permute-start | bytes 589832 | tf_op jit(solution)/shard_map/ppermute | solution.py:17
  265.0 7.2 collective-permute-start.1
  272.2 0.9 fusion.97
  273.1 14.7 %collective-permute-done = bf16[3,64,512]{2,1,0:T(8,128)(2,1)S(1)} collective-permute-done((bf16[3,64,512]{2,1,0:T(8,128)(2,1)S(1)}, bf16[3,64,512]{2,1,0:T(8,128)(2,1)S(1)}, u32[]{:S(2)}, u32[]{:S(2)}) %collective-permute-start) | collective-permute-done | bytes 196640 | tf_op jit(solution)/shard_map/ppermute | solution.py:17
  287.8 10.1 %collective-permute-done.1 = bf16[3,64,512]{2,1,0:T(8,128)(2,1)S(1)} collective-permute-done((bf16[3,64,512]{2,1,0:T(8,128)(2,1)S(1)}, bf16[3,64,512]{2,1,0:T(8,128)(2,1)S(1)}, u32[]{:S(2)}, u32[]{:S(2)}) %collective-permute-start.1) | collective-permute-done | bytes 196640 | tf_op jit(solution)/shard_map/ppermute | solution.py:20
  297.9 0.2 fusion.73
  298.1 4.0 add_convert_fusion.1
  302.1 90.6 %all-gather.8.cloned.1.call-done = bf16[1024,512]{0,1:T(8,128)(2,1)} async-done(((bf16[1024,8]{0,1:T(8,128)(2,1)}), bf16[1024,512]{0,1:T(8,128)(2,1)}) %all-gather.8.cloned.1.call-update) | async-done | bytes 1048592 | tf_op jit(solution)/shard_map/all_gather | solution.py:123
  392.6 1.7 convolution_convert_fusion
  394.3 1.2 copy.47
  395.6 12.2 %all-to-all-start = ((bf16[4,64,1024]{2,0,1:T(4,128)(2,1)}), bf16[4,64,1024]{2,0,1:T(4,128)(2,1)S(1)}, u32[]{:S(2)}, u32[]{:S(2)}) async-start(bf16[4,64,1024]{2,0,1:T(4,128)(2,1)} %copy.47), calls=%async_computation | async-start | bytes 1048576 | tf_op jit(solution)/shard_map/all_to_all | solution.py:144
  407.8 0.7 broadcast_in_dim.33
  408.5 119.2 %all_gather.18 = bf16[256,1024]{0,1:T(8,128)(2,1)S(1)} all-gather(bf16[256,16]{0,1:T(8,128)(2,1)S(1)} %copy-done.8), channel_id=1, replica_groups=mesh['row'=64,'col'=8] {'row'}, dimensions={1}, use_global_device_ids=true | all-gather | bytes 532480 | tf_op jit(solution)/shard_map/all_gather | solution.py:125
  527.7 0.2 copy.55
  527.9 118.3 %all_gather.19 = bf16[256,1024]{0,1:T(8,128)(2,1)S(1)} all-gather(bf16[256,16]{0,1:T(8,128)(2,1)S(1)} %copy-done.9), channel_id=1, replica_groups=mesh['row'=64,'col'=8] {'row'}, dimensions={1}, use_global_device_ids=true | all-gather | bytes 532480 | tf_op jit(solution)/shard_map/all_gather | solution.py:124
  646.3 1.0 copy.56
  647.3 0.2 convert_reduce_fusion.1
  647.5 0.4 fusion.63
  647.9 0.7 fusion.98
  648.5 0.2 convert_bitcast_fusion.1
  648.8 0.9 reshape.132
  649.7 1.5 copy.50
  651.2 1.9 reshape.128
  653.2 0.9 multiply_reduce_fusion
  654.1 0.5 fusion.58
  654.6 0.2 copy.51
  654.8 0.2 copy.58
  655.1 1.5 fusion.62
  656.6 13.0 %while.2 = (s32[]{:T(128)}, bf16[2,512,256]{2,1,0:T(8,128)(2,1)}, bf16[2,512,256]{2,1,0:T(8,128)(2,1)}, f32[256]{0:T(256)S(1)}, bf16[2,512,256]{2,1,0:T(8,128)(2...) while((s32[]{:T(128)}, bf16[2,512,256]{2,1,0:T(8,128)(2,1)}, ...), condition=%wide.region_13.14_spmd, body=%wide.region_8.13_spmd.sunk | while | flops 815006208 | bytes 10033349 | solution.py:60
  656.6 1.0 constant_dynamic-slice_fusion.2
  657.6 0.1 copy.67
  657.9 1.4 fusion.126
  659.4 2.7 fusion.127
  662.4 0.7 constant_dynamic-update-slice_fusion.2
  663.1 1.0 constant_dynamic-slice_fusion.2
  664.1 0.1 copy.67
  664.4 1.4 fusion.126
  665.9 2.7 fusion.127
  668.9 0.7 constant_dynamic-update-slice_fusion.2
  669.7 0.8 fusion.93
  670.6 2.2 collective-permute-start.2
  672.8 3.3 collective-permute-start.3
  676.2 1.5 collective-permute-done.3
  677.6 1.1 pad_maximum_fusion.7
  678.8 14.1 %collective-permute-start.4 = (bf16[70,3,256]{2,1,0:T(4,128)(2,1)S(1)}, bf16[70,3,256]{2,1,0:T(4,128)(2,1)S(1)}, u32[]{:S(2)}, u32[]{:S(2)}) collective-permute-start(bf16[70,3,256]{2,1,0:T(4,128)(2,1)S(1)} %get-tuple-element.157), channel_id=1, source_target_pairs={{1,0},{2,1},{3,2},{4,3},{5,4},{6,5},{7,6},{9,8},{10,9},{11,10},{12... | collective-permute-start | bytes 322568 | tf_op jit(solution)/shard_map/ppermute | solution.py:20
  692.9 1.9 collective-permute-start.5
  694.9 2.2 collective-permute-done.4
  697.0 13.1 %collective-permute-done.5 = bf16[70,3,256]{2,1,0:T(4,128)(2,1)S(1)} collective-permute-done((bf16[70,3,256]{2,1,0:T(4,128)(2,1)S(1)}, bf16[70,3,256]{2,1,0:T(4,128)(2,1)S(1)}, u32[]{:S(2)}, u32[]{:S(2)}) %collective-permute-start.5) | collective-permute-done | bytes 107552 | tf_op jit(solution)/shard_map/ppermute | solution.py:17
  710.1 1.7 pad_maximum_fusion
  712.0 11.3 %add_convert_fusion = bf16[64,16,256]{2,1,0:T(8,128)(2,1)} fusion(bf16[64,16,256]{2,1,0:T(8,128)(2,1)S(1)} %bitcast.207, bf16[64,16,256]{2,1,0:T(8,128)(2,1)} %fusion.62, bf16[3,16,256]{2,1,0:T(8,128)(2,1)S(1)} %collective-permute-done.2, bf16[3,16,256]{2,1,0:T(8,128)(2,1)S(1)} %collective-permute-done.3, bf16[70,19,256]{2,1,0:T(8,128)(2,1)S(1)} %get-tuple-element.156, ...), kind=kLoop, calls=%fused_computation.77 | loop fusion | flops 40632320 | bytes 23692288 | tf_op jit(solution)/shard_map/convert_element_type | solution.py:168
  (104 shorter events, 1.7 us)
Async XLA Ops:
  6.5 127.2 %all-gather.6.cloned.1.call-start = ((), (), s32[]{:S(2)}) async-start(), calls=%async_computation.2 | async-start | bytes 2129920 | tf_op jit(solution)/shard_map/all_gather | solution.py:121
  7.3 245.1 %all-gather.4.cloned.1.call-start = ((), (), s32[]{:S(2)}) async-start(), calls=%async_computation.1 | async-start | bytes 2129920 | tf_op jit(solution)/shard_map/all_gather | solution.py:122
  8.0 384.6 %all-gather.8.cloned.1.call-start = ((), (), s32[]{:S(2)}) async-start(), calls=%async_computation.3 | async-start | bytes 1064960 | tf_op jit(solution)/shard_map/all_gather | solution.py:123
  15.6 236.8 %copy-start.2 = (bf16[4,64,512]{2,1,0:T(8,128)(2,1)S(1)}, bf16[4,64,512]{2,1,0:T(8,128)(2,1)}, u32[]{:S(2)}) copy-start(bf16[4,64,512]{2,1,0:T(8,128)(2,1)} %param.23) | copy-start | bytes 786436
  15.6 236.8 %copy-start.25 = (f32[512]{0:T(512)S(1)}, f32[512]{0:T(512)}, u32[]{:S(2)}) copy-start(f32[512]{0:T(512)} %param.25) | copy-start | bytes 6148
  133.7 118.6 %copy-start.3 = (bf16[512,2048]{0,1:T(8,128)(2,1)S(1)}, bf16[512,2048]{0,1:T(8,128)(2,1)}, u32[]{:S(2)}) copy-start(bf16[512,2048]{0,1:T(8,128)(2,1)} %all-gather.6.cloned.1.call-done) | copy-start | bytes 6291460
  256.4 41.6 %copy-start.4 = (bf16[4,64,512]{2,1,0:T(8,128)(2,1)S(1)}, bf16[4,64,512]{2,1,0:T(8,128)(2,1)}, u32[]{:S(2)}) copy-start(bf16[4,64,512]{2,1,0:T(8,128)(2,1)} %param.24) | copy-start | bytes 786436
  256.7 31.1 %collective-permute-start = (bf16[3,64,512]{2,1,0:T(8,128)(2,1)S(1)}, bf16[3,64,512]{2,1,0:T(8,128)(2,1)S(1)}, u32[]{:S(2)}, u32[]{:S(2)}) collective-permute-start(bf16[3,64,512]{2,1,0:T(8,128)(2,1)S(1)} %bitcast.212), channel_id=1, source_target_pairs={{0,1},{1,2},{2,3},{3,4},{4,5},{5,6},{6,7},{7,8},{8,9},{9,10},{10,1... | collective-permute-start | bytes 589832 | tf_op jit(solution)/shard_map/ppermute | solution.py:17
  265.0 32.9 %collective-permute-start.1 = (bf16[3,64,512]{2,1,0:T(8,128)(2,1)S(1)}, bf16[3,64,512]{2,1,0:T(8,128)(2,1)S(1)}, u32[]{:S(2)}, u32[]{:S(2)}) collective-permute-start(bf16[3,64,512]{2,1,0:T(8,128)(2,1)S(1)} %bitcast.211), channel_id=1, source_target_pairs={{1,0},{2,1},{3,2},{4,3},{5,4},{6,5},{7,6},{8,7},{9,8},{10,9},{11,1... | collective-permute-start | bytes 589832 | tf_op jit(solution)/shard_map/ppermute | solution.py:20
  302.1 105.7 %copy-start.30 = (s32[4,1]{0,1:T(1,128)S(1)}, s32[4,1]{0,1:T(1,128)}, u32[]{:S(2)}) copy-start(s32[4,1]{0,1:T(1,128)} %param.43) | copy-start | bytes 52
  302.1 106.4 %copy-start.8 = (bf16[256,16]{0,1:T(8,128)(2,1)S(1)}, bf16[256,16]{0,1:T(8,128)(2,1)}, u32[]{:S(2)}) copy-start(bf16[256,16]{0,1:T(8,128)(2,1)} %param.42) | copy-start | bytes 24580
  394.3 133.6 %copy-start.9 = (bf16[256,16]{0,1:T(8,128)(2,1)S(1)}, bf16[256,16]{0,1:T(8,128)(2,1)}, u32[]{:S(2)}) copy-start(bf16[256,16]{0,1:T(8,128)(2,1)} %param.41) | copy-start | bytes 24580
  395.5 251.7 %copy-start = (bf16[64,16,256]{2,1,0:T(8,128)(2,1)S(1)}, bf16[64,16,256]{2,1,0:T(8,128)(2,1)}, u32[]{:S(2)}) copy-start(bf16[64,16,256]{2,1,0:T(8,128)(2,1)} %param.34) | copy-start | bytes 1572868
  395.6 253.0 %all-to-all-start = ((bf16[4,64,1024]{2,0,1:T(4,128)(2,1)}), bf16[4,64,1024]{2,0,1:T(4,128)(2,1)S(1)}, u32[]{:S(2)}, u32[]{:S(2)}) async-start(bf16[4,64,1024]{2,0,1:T(4,128)(2,1)} %copy.47), calls=%async_computation | async-start | bytes 1048576 | tf_op jit(solution)/shard_map/all_to_all | solution.py:144
  408.5 239.4 %copy-start.5 = (f32[7,7,256]{2,1,0:T(8,128)S(1)}, f32[7,7,256]{2,1,0:T(8,128)}, u32[]{:S(2)}) copy-start(f32[7,7,256]{2,1,0:T(8,128)} %param.40) | copy-start | bytes 150532
  649.7 3.5 copy-start.7
  654.0 1.1 copy-start.26
  654.1 2.6 copy-start.6
  657.6 1.8 copy-start.27
  657.6 1.8 copy-start.28
  657.6 1.8 copy-start.29
  664.1 1.8 copy-start.27
  664.1 1.8 copy-start.28
  664.1 1.8 copy-start.29
  669.6 42.2 %copy-start.1 = (bf16[2,512,256]{2,1,0:T(8,128)(2,1)S(1)}, bf16[2,512,256]{2,1,0:T(8,128)(2,1)}, u32[]{:S(2)}) copy-start(bf16[2,512,256]{2,1,0:T(8,128)(2,1)} %get-tuple-element.87) | copy-start | bytes 1572868
  669.6 42.2 %copy-start.10 = (f32[1,1,256]{2,1,0:T(1,128)S(1)}, f32[1,1,256]{2,1,0:T(1,128)}, u32[]{:S(2)}) copy-start(f32[1,1,256]{2,1,0:T(1,128)} %get-tuple-element.216) | copy-start | bytes 3076
  669.6 42.2 %copy-start.11 = (f32[1,1,256]{2,1,0:T(1,128)S(1)}, f32[1,1,256]{2,1,0:T(1,128)}, u32[]{:S(2)}) copy-start(f32[1,1,256]{2,1,0:T(1,128)} %get-tuple-element.217) | copy-start | bytes 3076
  669.6 42.2 %copy-start.12 = (f32[1,1,256]{2,1,0:T(1,128)S(1)}, f32[1,1,256]{2,1,0:T(1,128)}, u32[]{:S(2)}) copy-start(f32[1,1,256]{2,1,0:T(1,128)} %get-tuple-element.218) | copy-start | bytes 3076
  669.6 42.3 %copy-start.13 = (f32[1,1,256]{2,1,0:T(1,128)S(1)}, f32[1,1,256]{2,1,0:T(1,128)}, u32[]{:S(2)}) copy-start(f32[1,1,256]{2,1,0:T(1,128)} %get-tuple-element.219) | copy-start | bytes 3076
  669.6 42.3 %copy-start.14 = (f32[1,1,256]{2,1,0:T(1,128)S(1)}, f32[1,1,256]{2,1,0:T(1,128)}, u32[]{:S(2)}) copy-start(f32[1,1,256]{2,1,0:T(1,128)} %get-tuple-element.220) | copy-start | bytes 3076
  669.6 42.3 %copy-start.15 = (f32[1,1,256]{2,1,0:T(1,128)S(1)}, f32[1,1,256]{2,1,0:T(1,128)}, u32[]{:S(2)}) copy-start(f32[1,1,256]{2,1,0:T(1,128)} %get-tuple-element.221) | copy-start | bytes 3076
  669.7 42.3 %copy-start.16 = (f32[1,1,256]{2,1,0:T(1,128)S(1)}, f32[1,1,256]{2,1,0:T(1,128)}, u32[]{:S(2)}) copy-start(f32[1,1,256]{2,1,0:T(1,128)} %get-tuple-element.222) | copy-start | bytes 3076
  669.7 42.3 %copy-start.17 = (f32[1,1,256]{2,1,0:T(1,128)S(1)}, f32[1,1,256]{2,1,0:T(1,128)}, u32[]{:S(2)}) copy-start(f32[1,1,256]{2,1,0:T(1,128)} %get-tuple-element.223) | copy-start | bytes 3076
  669.7 42.3 %copy-start.18 = (f32[1,1,256]{2,1,0:T(1,128)S(1)}, f32[1,1,256]{2,1,0:T(1,128)}, u32[]{:S(2)}) copy-start(f32[1,1,256]{2,1,0:T(1,128)} %get-tuple-element.224) | copy-start | bytes 3076
  669.7 42.3 %copy-start.19 = (f32[1,1,256]{2,1,0:T(1,128)S(1)}, f32[1,1,256]{2,1,0:T(1,128)}, u32[]{:S(2)}) copy-start(f32[1,1,256]{2,1,0:T(1,128)} %get-tuple-element.225) | copy-start | bytes 3076
  669.7 42.3 %copy-start.20 = (f32[1,1,256]{2,1,0:T(1,128)S(1)}, f32[1,1,256]{2,1,0:T(1,128)}, u32[]{:S(2)}) copy-start(f32[1,1,256]{2,1,0:T(1,128)} %get-tuple-element.226) | copy-start | bytes 3076
  669.7 42.3 %copy-start.21 = (f32[1,1,256]{2,1,0:T(1,128)S(1)}, f32[1,1,256]{2,1,0:T(1,128)}, u32[]{:S(2)}) copy-start(f32[1,1,256]{2,1,0:T(1,128)} %get-tuple-element.227) | copy-start | bytes 3076
  669.7 42.3 %copy-start.22 = (f32[1,1,256]{2,1,0:T(1,128)S(1)}, f32[1,1,256]{2,1,0:T(1,128)}, u32[]{:S(2)}) copy-start(f32[1,1,256]{2,1,0:T(1,128)} %get-tuple-element.228) | copy-start | bytes 3076
  669.7 42.3 %copy-start.23 = (f32[1,1,256]{2,1,0:T(1,128)S(1)}, f32[1,1,256]{2,1,0:T(1,128)}, u32[]{:S(2)}) copy-start(f32[1,1,256]{2,1,0:T(1,128)} %get-tuple-element.229) | copy-start | bytes 3076
  669.7 42.3 %copy-start.24 = (f32[1,1,256]{2,1,0:T(1,128)S(1)}, f32[1,1,256]{2,1,0:T(1,128)}, u32[]{:S(2)}) copy-start(f32[1,1,256]{2,1,0:T(1,128)} %get-tuple-element.230) | copy-start | bytes 3076
  670.6 5.6 collective-permute-start.2
  672.8 4.8 collective-permute-start.3
  678.8 18.2 %collective-permute-start.4 = (bf16[70,3,256]{2,1,0:T(4,128)(2,1)S(1)}, bf16[70,3,256]{2,1,0:T(4,128)(2,1)S(1)}, u32[]{:S(2)}, u32[]{:S(2)}) collective-permute-start(bf16[70,3,256]{2,1,0:T(4,128)(2,1)S(1)} %get-tuple-element.157), channel_id=1, source_target_pairs={{1,0},{2,1},{3,2},{4,3},{5,4},{6,5},{7,6},{9,8},{10,9},{11,10},{12... | collective-permute-start | bytes 322568 | tf_op jit(solution)/shard_map/ppermute | solution.py:20
  692.9 17.2 %collective-permute-start.5 = (bf16[70,3,256]{2,1,0:T(4,128)(2,1)S(1)}, bf16[70,3,256]{2,1,0:T(4,128)(2,1)S(1)}, u32[]{:S(2)}, u32[]{:S(2)}) collective-permute-start(bf16[70,3,256]{2,1,0:T(4,128)(2,1)S(1)} %get-tuple-element.158), channel_id=1, source_target_pairs={{0,1},{1,2},{2,3},{3,4},{4,5},{5,6},{6,7},{8,9},{9,10},{10,11},{11... | collective-permute-start | bytes 322568 | tf_op jit(solution)/shard_map/ppermute | solution.py:17
Sparse Core Ops, SparseCore 0:
  9.5 124.2 all-gather.5
  135.9 116.3 all-gather.3
  254.5 138.1 all-gather.7
where the time goes:
time: 731 us; the launch traced here: 730 us
  waiting for transfers between devices  367 us (50%)
  blocking collectives  238 us (33%)
  starting transfers between devices  49.3 us (7%)
  other arithmetic  27.2 us (4%)
  matrix products  17.8 us (2%)
  local copies, waits for them, and re-layouts  17.1 us (2%)
  between operations  13.7 us (2%)
    all_gather x1, blocking collectives, on_device(): lax.all_gather(project2, 'row', axis=1, tiled=True)  119 us
    all_gather x1, blocking collectives, on_device(): lax.all_gather(expand2, 'row', axis=1, tiled=True)  118 us
    all_gather x1, waiting for transfers between devices, on_device(): lax.all_gather(expand3, 'row', axis=1, tiled=True)  118 us
    all_gather x1, waiting for transfers between devices, on_device(): lax.all_gather(project3, 'row', axis=1, tiled=True)  115 us
    all_gather x1, waiting for transfers between devices, on_device(): lax.all_gather(down_w, 'row', axis=1, tiled=True)  90.6 us
    ppermute x3, waiting for transfers between devices, padded_2(): lax.ppermute(lax.slice_in_dim(block, block.shape[dim] - width, None, axis...  27.8 us
    ppermute x3, starting transfers between devices, padded_2(): lax.ppermute(lax.slice_in_dim(block, 0, width, axis=dim), axis, backward)  24.6 us
  transfers between devices with their start and end apart: 10, of which 8 were waited for; matrix products, arithmetic and copies ran while one was open for 3% of the time, Pallas kernels for 0%

commit v1 on v0

--- a/solution.py
+++ b/solution.py
@@ -7,6 +7,13 @@
 EPS = 1e-06
 ROOT_HALF = 0.7071067811865476
 DENS = 0.3989422804014327
+
+
+def raise_the_slots(m, lane_axis):
+    passed = jnp.stack([m for _ in range(lax.axis_size(lane_axis))])
+    return jnp.concatenate(
+        lax.all_to_all(passed, axis_name=lane_axis, split_axis=0, concat_axis=0), axis=1
+    )
 
 
 def padded_2(block, sides, width):
@@ -121,7 +128,7 @@
         lax.all_gather(expand3, "row", axis=1, tiled=True),
         lax.all_gather(project3, "row", axis=1, tiled=True),
         lax.all_gather(down_w, "row", axis=1, tiled=True),
-        lax.all_gather(expand2, "row", axis=1, tiled=True),
+        raise_the_slots(expand2, "row"),
         lax.all_gather(project2, "row", axis=1, tiled=True),
     )
     rows3, width3, chans3 = u3.shape

time: 731 us -> 623 us (0.85)
  blocking collectives: 238 us -> 122 us
  starting transfers between devices: 49.3 us -> 66.9 us
  waiting for transfers between devices: 367 us -> 357 us
    all_gather x1 -> x0, blocking collectives: 118 us -> none  [on_device(): lax.all_gather(expand2, 'row', axis=1, tiled=True)]
    all_to_all x0 -> x1, starting transfers between devices: none -> 16.1 us  [raise_the_slots(): lax.all_to_all(passed, axis_name=lane_axis, split_axis=0, concat_axis=0)]
    all_gather x1, waiting for transfers between devices: 118 us -> 107 us  [on_device(): lax.all_gather(expand3, 'row', axis=1, tiled=True)]
  transfers between devices with their start and end apart: 10 -> 11, of which waited for: 8 -> 8; matrix products, arithmetic and copies ran while one was open for 3% -> 4% of each run, Pallas kernels for 0% -> 0%
where the time goes in v1:
time: 623 us; the launch traced here: 622 us
  waiting for transfers between devices  357 us (57%)
  blocking collectives  122 us (20%)
  starting transfers between devices  66.9 us (11%)
  other arithmetic  26.1 us (4%)
  matrix products  18.6 us (3%)
  local copies, waits for them, and re-layouts  16.9 us (3%)
  between operations  14.2 us (2%)
    all_gather x1, blocking collectives, on_device(): lax.all_gather(project2, 'row', axis=1, tiled=True)  122 us
    all_gather x1, waiting for transfers between devices, on_device(): lax.all_gather(project3, 'row', axis=1, tiled=True)  117 us
    all_gather x1, waiting for transfers between devices, on_device(): lax.all_gather(expand3, 'row', axis=1, tiled=True)  107 us
    all_gather x1, waiting for transfers between devices, on_device(): lax.all_gather(down_w, 'row', axis=1, tiled=True)  89.9 us
    ppermute x3, waiting for transfers between devices, padded_2(): lax.ppermute(lax.slice_in_dim(block, block.shape[dim] - width, None, axis...  28.4 us
    ppermute x3, starting transfers between devices, padded_2(): lax.ppermute(lax.slice_in_dim(block, 0, width, axis=dim), axis, backward)  24.4 us
    all_to_all x1, starting transfers between devices, raise_the_slots(): lax.all_to_all(passed, axis_name=lane_axis, split_axis=0, concat_axis=0)  16.1 us
    ppermute x3, starting transfers between devices, padded_2(): lax.ppermute(lax.slice_in_dim(block, block.shape[dim] - width, None, axis...  14.2 us
  transfers between devices with their start and end apart: 11, of which 8 were waited for; matrix products, arithmetic and copies ran while one was open for 4% of the time, Pallas kernels for 0%

profile of v1, /device:TPU:10, one launch (start us, length us, event | category | flops | bytes accessed | tf_op | source)
XLA Modules:
  0.0 622.1 jit_solution(12136753431146917190)
XLA Ops:
  6.6 0.7 all-gather.6.cloned.1.call-update
  7.4 0.7 all-gather.4.cloned.1.call-update
  8.1 1.6 stack.2
  9.6 16.1 %all-to-all-start.1 = ((bf16[64,256,16]{1,2,0:T(8,128)(2,1)}), bf16[64,256,16]{1,2,0:T(8,128)(2,1)S(1)}, u32[]{:S(2)}, u32[]{:S(2)}) async-start(bf16[64,256,16]{1,2,0:T(8,128)(2,1)} %stack.2), calls=%async_computation.1 | async-start | bytes 1048576 | tf_op jit(solution)/shard_map/all_to_all | solution.py:15
  25.8 0.7 all-gather.8.cloned.1.call-update
  26.5 1.1 convert_reduce_fusion.2
  27.5 0.2 multiply_reduce_fusion.2
  27.8 0.7 fusion.96
  28.5 0.7 fusion.95
  29.3 0.8 fusion.79
  30.0 0.2 add_convert_fusion.2
  30.2 107.1 %all-gather.6.cloned.1.call-done = bf16[512,2048]{0,1:T(8,128)(2,1)} async-done(((bf16[512,32]{0,1:T(8,128)(2,1)}), bf16[512,2048]{0,1:T(8,128)(2,1)}) %all-gather.6.cloned.1.call-update) | async-done | bytes 2097168 | tf_op jit(solution)/shard_map/all_gather | solution.py:128
  137.3 3.8 convolution_add_fusion
  141.2 117.0 %all-gather.4.cloned.1.call-done = bf16[512,2048]{0,1:T(8,128)(2,1)} async-done(((bf16[512,32]{0,1:T(8,128)(2,1)}), bf16[512,2048]{0,1:T(8,128)(2,1)}) %all-gather.4.cloned.1.call-update) | async-done | bytes 2097168 | tf_op jit(solution)/shard_map/all_gather | solution.py:129
  258.2 4.9 fusion.90
  263.4 1.3 multiply_convert_fusion
  264.7 8.2 %collective-permute-start = (bf16[3,64,512]{2,1,0:T(8,128)(2,1)S(1)}, bf16[3,64,512]{2,1,0:T(8,128)(2,1)S(1)}, u32[]{:S(2)}, u32[]{:S(2)}) collective-permute-start(bf16[3,64,512]{2,1,0:T(8,128)(2,1)S(1)} %bitcast.216), channel_id=1, source_target_pairs={{0,1},{1,2},{2,3},{3,4},{4,5},{5,6},{6,7},{7,8},{8,9},{9,10},{10,1... | collective-permute-start | bytes 589832 | tf_op jit(solution)/shard_map/ppermute | solution.py:24
  273.0 7.2 %collective-permute-start.1 = (bf16[3,64,512]{2,1,0:T(8,128)(2,1)S(1)}, bf16[3,64,512]{2,1,0:T(8,128)(2,1)S(1)}, u32[]{:S(2)}, u32[]{:S(2)}) collective-permute-start(bf16[3,64,512]{2,1,0:T(8,128)(2,1)S(1)} %bitcast.215), channel_id=1, source_target_pairs={{1,0},{2,1},{3,2},{4,3},{5,4},{6,5},{7,6},{8,7},{9,8},{10,9},{11,1... | collective-permute-start | bytes 589832 | tf_op jit(solution)/shard_map/ppermute | solution.py:27
  280.2 15.8 %collective-permute-done = bf16[3,64,512]{2,1,0:T(8,128)(2,1)S(1)} collective-permute-done((bf16[3,64,512]{2,1,0:T(8,128)(2,1)S(1)}, bf16[3,64,512]{2,1,0:T(8,128)(2,1)S(1)}, u32[]{:S(2)}, u32[]{:S(2)}) %collective-permute-start) | collective-permute-done | bytes 196640 | tf_op jit(solution)/shard_map/ppermute | solution.py:24
  296.0 10.4 %collective-permute-done.1 = bf16[3,64,512]{2,1,0:T(8,128)(2,1)S(1)} collective-permute-done((bf16[3,64,512]{2,1,0:T(8,128)(2,1)S(1)}, bf16[3,64,512]{2,1,0:T(8,128)(2,1)S(1)}, u32[]{:S(2)}, u32[]{:S(2)}) %collective-permute-start.1) | collective-permute-done | bytes 196640 | tf_op jit(solution)/shard_map/ppermute | solution.py:27
  306.4 0.2 fusion.73
  307.0 4.0 add_convert_fusion.1
  311.0 89.9 %all-gather.8.cloned.1.call-done = bf16[1024,512]{0,1:T(8,128)(2,1)} async-done(((bf16[1024,8]{0,1:T(8,128)(2,1)}), bf16[1024,512]{0,1:T(8,128)(2,1)}) %all-gather.8.cloned.1.call-update) | async-done | bytes 1048592 | tf_op jit(solution)/shard_map/all_gather | solution.py:130
  400.8 1.7 convolution_convert_fusion
  402.5 1.2 copy.47
  403.7 12.2 %all-to-all-start = ((bf16[4,64,1024]{2,0,1:T(4,128)(2,1)}), bf16[4,64,1024]{2,0,1:T(4,128)(2,1)S(1)}, u32[]{:S(2)}, u32[]{:S(2)}) async-start(bf16[4,64,1024]{2,0,1:T(4,128)(2,1)} %copy.47), calls=%async_computation | async-start | bytes 1048576 | tf_op jit(solution)/shard_map/all_to_all | solution.py:151
  416.0 0.6 broadcast_in_dim.33
  416.7 121.9 %all_gather.15 = bf16[256,1024]{0,1:T(8,128)(2,1)S(1)} all-gather(bf16[256,16]{0,1:T(8,128)(2,1)S(1)} %copy-done.10), channel_id=1, replica_groups=mesh['row'=64,'col'=8] {'row'}, dimensions={1}, use_global_device_ids=true | all-gather | bytes 532480 | tf_op jit(solution)/shard_map/all_gather | solution.py:132
  538.6 0.2 copy.55
  538.8 0.2 convert_reduce_fusion.1
  539.0 0.4 fusion.63
  539.4 0.7 fusion.98
  540.1 1.0 copy.56
  541.1 0.2 convert_bitcast_fusion.1
  541.3 0.9 reshape.142
  542.2 1.5 copy.50
  543.8 1.9 reshape.136
  545.7 0.9 multiply_reduce_fusion
  546.6 0.5 fusion.58
  547.1 0.2 copy.51
  547.3 0.2 copy.58
  547.7 1.5 fusion.62
  549.2 13.0 %while.2 = (s32[]{:T(128)}, bf16[2,512,256]{2,1,0:T(8,128)(2,1)}, bf16[2,512,256]{2,1,0:T(8,128)(2,1)}, f32[256]{0:T(256)S(1)}, bf16[2,512,256]{2,1,0:T(8,128)(2...) while((s32[]{:T(128)}, bf16[2,512,256]{2,1,0:T(8,128)(2,1)}, ...), condition=%wide.region_13.14_spmd, body=%wide.region_8.13_spmd.sunk | while | flops 815006208 | bytes 10033349 | solution.py:67
  549.2 1.0 constant_dynamic-slice_fusion.2
  550.2 0.1 copy.67
  550.5 1.4 fusion.126
  551.9 2.7 fusion.127
  554.9 0.7 constant_dynamic-update-slice_fusion.2
  555.7 1.0 constant_dynamic-slice_fusion.2
  556.7 0.1 copy.67
  557.0 1.4 fusion.126
  558.4 2.7 fusion.127
  561.4 0.7 constant_dynamic-update-slice_fusion.2
  562.3 0.8 fusion.93
  563.1 2.2 collective-permute-start.2
  565.4 6.0 collective-permute-start.3
  571.5 1.5 collective-permute-done.3
  572.9 1.1 pad_maximum_fusion.7
  574.1 11.1 %collective-permute-start.4 = (bf16[70,3,256]{2,1,0:T(4,128)(2,1)S(1)}, bf16[70,3,256]{2,1,0:T(4,128)(2,1)S(1)}, u32[]{:S(2)}, u32[]{:S(2)}) collective-permute-start(bf16[70,3,256]{2,1,0:T(4,128)(2,1)S(1)} %get-tuple-element.157), channel_id=1, source_target_pairs={{1,0},{2,1},{3,2},{4,3},{5,4},{6,5},{7,6},{9,8},{10,9},{11,10},{12... | collective-permute-start | bytes 322568 | tf_op jit(solution)/shard_map/ppermute | solution.py:27
  585.2 3.7 collective-permute-start.5
  588.9 0.9 collective-permute-done.4
  589.8 12.6 %collective-permute-done.5 = bf16[70,3,256]{2,1,0:T(4,128)(2,1)S(1)} collective-permute-done((bf16[70,3,256]{2,1,0:T(4,128)(2,1)S(1)}, bf16[70,3,256]{2,1,0:T(4,128)(2,1)S(1)}, u32[]{:S(2)}, u32[]{:S(2)}) %collective-permute-start.5) | collective-permute-done | bytes 107552 | tf_op jit(solution)/shard_map/ppermute | solution.py:24
  602.4 1.7 pad_maximum_fusion
  604.3 11.3 %add_convert_fusion = bf16[64,16,256]{2,1,0:T(8,128)(2,1)} fusion(bf16[64,16,256]{2,1,0:T(8,128)(2,1)S(1)} %bitcast.210, bf16[64,16,256]{2,1,0:T(8,128)(2,1)} %fusion.62, bf16[3,16,256]{2,1,0:T(8,128)(2,1)S(1)} %collective-permute-done.2, bf16[3,16,256]{2,1,0:T(8,128)(2,1)S(1)} %collective-permute-done.3, bf16[70,19,256]{2,1,0:T(8,128)(2,1)S(1)} %get-tuple-element.156, ...), kind=kLoop, calls=%fused_computation.77 | loop fusion | flops 40632320 | bytes 23692288 | tf_op jit(solution)/shard_map/convert_element_type | solution.py:175
  (180 shorter events, 1.9 us)
Async XLA Ops:
  6.6 130.8 %copy-start.9 = (f32[2048]{0:T(1024)S(1)}, f32[2048]{0:T(1024)}, u32[]{:S(2)}) copy-start(f32[2048]{0:T(1024)} %param.27) | copy-start | bytes 24580
  6.6 130.8 %all-gather.6.cloned.1.call-start = ((), (), s32[]{:S(2)}) async-start(), calls=%async_computation.3 | async-start | bytes 2129920 | tf_op jit(solution)/shard_map/all_gather | solution.py:128
  7.3 250.9 %all-gather.4.cloned.1.call-start = ((), (), s32[]{:S(2)}) async-start(), calls=%async_computation.2 | async-start | bytes 2129920 | tf_op jit(solution)/shard_map/all_gather | solution.py:129
  9.6 394.1 %all-to-all-start.1 = ((bf16[64,256,16]{1,2,0:T(8,128)(2,1)}), bf16[64,256,16]{1,2,0:T(8,128)(2,1)S(1)}, u32[]{:S(2)}, u32[]{:S(2)}) async-start(bf16[64,256,16]{1,2,0:T(8,128)(2,1)} %stack.2), calls=%async_computation.1 | async-start | bytes 1048576 | tf_op jit(solution)/shard_map/all_to_all | solution.py:15
  25.7 375.1 %all-gather.8.cloned.1.call-start = ((), (), s32[]{:S(2)}) async-start(), calls=%async_computation.4 | async-start | bytes 1064960 | tf_op jit(solution)/shard_map/all_gather | solution.py:130
  137.3 120.9 %copy-start.3 = (bf16[512,2048]{0,1:T(8,128)(2,1)S(1)}, bf16[512,2048]{0,1:T(8,128)(2,1)}, u32[]{:S(2)}) copy-start(bf16[512,2048]{0,1:T(8,128)(2,1)} %all-gather.6.cloned.1.call-done) | copy-start | bytes 6291460
  263.1 43.5 %copy-start.11 = (f32[1,1,512]{2,1,0:T(1,128)S(1)}, f32[1,1,512]{2,1,0:T(1,128)}, u32[]{:S(2)}) copy-start(f32[1,1,512]{2,1,0:T(1,128)} %get-tuple-element.186) | copy-start | bytes 6148
  263.1 43.5 %copy-start.12 = (f32[1,1,512]{2,1,0:T(1,128)S(1)}, f32[1,1,512]{2,1,0:T(1,128)}, u32[]{:S(2)}) copy-start(f32[1,1,512]{2,1,0:T(1,128)} %get-tuple-element.187) | copy-start | bytes 6148
  263.1 43.5 %copy-start.13 = (f32[1,1,512]{2,1,0:T(1,128)S(1)}, f32[1,1,512]{2,1,0:T(1,128)}, u32[]{:S(2)}) copy-start(f32[1,1,512]{2,1,0:T(1,128)} %get-tuple-element.188) | copy-start | bytes 6148
  263.1 43.6 %copy-start.14 = (f32[1,1,512]{2,1,0:T(1,128)S(1)}, f32[1,1,512]{2,1,0:T(1,128)}, u32[]{:S(2)}) copy-start(f32[1,1,512]{2,1,0:T(1,128)} %get-tuple-element.189) | copy-start | bytes 6148
  263.1 43.6 %copy-start.15 = (f32[1,1,512]{2,1,0:T(1,128)S(1)}, f32[1,1,512]{2,1,0:T(1,128)}, u32[]{:S(2)}) copy-start(f32[1,1,512]{2,1,0:T(1,128)} %get-tuple-element.190) | copy-start | bytes 6148
  263.1 43.6 %copy-start.16 = (f32[1,1,512]{2,1,0:T(1,128)S(1)}, f32[1,1,512]{2,1,0:T(1,128)}, u32[]{:S(2)}) copy-start(f32[1,1,512]{2,1,0:T(1,128)} %get-tuple-element.191) | copy-start | bytes 6148
  263.1 43.6 %copy-start.17 = (f32[1,1,512]{2,1,0:T(1,128)S(1)}, f32[1,1,512]{2,1,0:T(1,128)}, u32[]{:S(2)}) copy-start(f32[1,1,512]{2,1,0:T(1,128)} %get-tuple-element.192) | copy-start | bytes 6148
  263.2 43.6 %copy-start.18 = (f32[1,1,512]{2,1,0:T(1,128)S(1)}, f32[1,1,512]{2,1,0:T(1,128)}, u32[]{:S(2)}) copy-start(f32[1,1,512]{2,1,0:T(1,128)} %get-tuple-element.193) | copy-start | bytes 6148
  263.2 43.6 %copy-start.19 = (f32[1,1,512]{2,1,0:T(1,128)S(1)}, f32[1,1,512]{2,1,0:T(1,128)}, u32[]{:S(2)}) copy-start(f32[1,1,512]{2,1,0:T(1,128)} %get-tuple-element.194) | copy-start | bytes 6148
  263.2 43.6 %copy-start.20 = (f32[1,1,512]{2,1,0:T(1,128)S(1)}, f32[1,1,512]{2,1,0:T(1,128)}, u32[]{:S(2)}) copy-start(f32[1,1,512]{2,1,0:T(1,128)} %get-tuple-element.195) | copy-start | bytes 6148
  263.2 43.6 %copy-start.21 = (f32[1,1,512]{2,1,0:T(1,128)S(1)}, f32[1,1,512]{2,1,0:T(1,128)}, u32[]{:S(2)}) copy-start(f32[1,1,512]{2,1,0:T(1,128)} %get-tuple-element.196) | copy-start | bytes 6148
  263.2 43.6 %copy-start.22 = (f32[1,1,512]{2,1,0:T(1,128)S(1)}, f32[1,1,512]{2,1,0:T(1,128)}, u32[]{:S(2)}) copy-start(f32[1,1,512]{2,1,0:T(1,128)} %get-tuple-element.197) | copy-start | bytes 6148
  263.2 43.6 %copy-start.23 = (f32[1,1,512]{2,1,0:T(1,128)S(1)}, f32[1,1,512]{2,1,0:T(1,128)}, u32[]{:S(2)}) copy-start(f32[1,1,512]{2,1,0:T(1,128)} %get-tuple-element.198) | copy-start | bytes 6148
  263.2 43.6 %copy-start.24 = (f32[1,1,512]{2,1,0:T(1,128)S(1)}, f32[1,1,512]{2,1,0:T(1,128)}, u32[]{:S(2)}) copy-start(f32[1,1,512]{2,1,0:T(1,128)} %get-tuple-element.199) | copy-start | bytes 6148
  263.2 43.6 %copy-start.25 = (f32[1,1,512]{2,1,0:T(1,128)S(1)}, f32[1,1,512]{2,1,0:T(1,128)}, u32[]{:S(2)}) copy-start(f32[1,1,512]{2,1,0:T(1,128)} %get-tuple-element.200) | copy-start | bytes 6148
  263.2 43.6 %copy-start.26 = (f32[1,1,512]{2,1,0:T(1,128)S(1)}, f32[1,1,512]{2,1,0:T(1,128)}, u32[]{:S(2)}) copy-start(f32[1,1,512]{2,1,0:T(1,128)} %get-tuple-element.163) | copy-start | bytes 6148
  263.2 43.6 %copy-start.27 = (f32[1,1,512]{2,1,0:T(1,128)S(1)}, f32[1,1,512]{2,1,0:T(1,128)}, u32[]{:S(2)}) copy-start(f32[1,1,512]{2,1,0:T(1,128)} %get-tuple-element.164) | copy-start | bytes 6148
  263.3 43.6 %copy-start.28 = (f32[1,1,512]{2,1,0:T(1,128)S(1)}, f32[1,1,512]{2,1,0:T(1,128)}, u32[]{:S(2)}) copy-start(f32[1,1,512]{2,1,0:T(1,128)} %get-tuple-element.165) | copy-start | bytes 6148
  263.3 43.6 %copy-start.29 = (f32[1,1,512]{2,1,0:T(1,128)S(1)}, f32[1,1,512]{2,1,0:T(1,128)}, u32[]{:S(2)}) copy-start(f32[1,1,512]{2,1,0:T(1,128)} %get-tuple-element.166) | copy-start | bytes 6148
  263.3 43.6 %copy-start.30 = (f32[1,1,512]{2,1,0:T(1,128)S(1)}, f32[1,1,512]{2,1,0:T(1,128)}, u32[]{:S(2)}) copy-start(f32[1,1,512]{2,1,0:T(1,128)} %get-tuple-element.167) | copy-start | bytes 6148
  263.3 43.6 %copy-start.31 = (f32[1,1,512]{2,1,0:T(1,128)S(1)}, f32[1,1,512]{2,1,0:T(1,128)}, u32[]{:S(2)}) copy-start(f32[1,1,512]{2,1,0:T(1,128)} %get-tuple-element.168) | copy-start | bytes 6148
  263.3 43.6 %copy-start.32 = (f32[1,1,512]{2,1,0:T(1,128)S(1)}, f32[1,1,512]{2,1,0:T(1,128)}, u32[]{:S(2)}) copy-start(f32[1,1,512]{2,1,0:T(1,128)} %get-tuple-element.169) | copy-start | bytes 6148
  263.3 43.6 %copy-start.33 = (f32[1,1,512]{2,1,0:T(1,128)S(1)}, f32[1,1,512]{2,1,0:T(1,128)}, u32[]{:S(2)}) copy-start(f32[1,1,512]{2,1,0:T(1,128)} %get-tuple-element.170) | copy-start | bytes 6148
  263.3 43.6 %copy-start.34 = (f32[1,1,512]{2,1,0:T(1,128)S(1)}, f32[1,1,512]{2,1,0:T(1,128)}, u32[]{:S(2)}) copy-start(f32[1,1,512]{2,1,0:T(1,128)} %get-tuple-element.171) | copy-start | bytes 6148
  263.3 43.6 %copy-start.35 = (f32[1,1,512]{2,1,0:T(1,128)S(1)}, f32[1,1,512]{2,1,0:T(1,128)}, u32[]{:S(2)}) copy-start(f32[1,1,512]{2,1,0:T(1,128)} %get-tuple-element.172) | copy-start | bytes 6148
  263.3 43.6 %copy-start.36 = (f32[1,1,512]{2,1,0:T(1,128)S(1)}, f32[1,1,512]{2,1,0:T(1,128)}, u32[]{:S(2)}) copy-start(f32[1,1,512]{2,1,0:T(1,128)} %get-tuple-element.173) | copy-start | bytes 6148
  263.3 43.6 %copy-start.37 = (f32[1,1,512]{2,1,0:T(1,128)S(1)}, f32[1,1,512]{2,1,0:T(1,128)}, u32[]{:S(2)}) copy-start(f32[1,1,512]{2,1,0:T(1,128)} %get-tuple-element.174) | copy-start | bytes 6148
  263.4 43.6 %copy-start.38 = (f32[1,1,512]{2,1,0:T(1,128)S(1)}, f32[1,1,512]{2,1,0:T(1,128)}, u32[]{:S(2)}) copy-start(f32[1,1,512]{2,1,0:T(1,128)} %get-tuple-element.175) | copy-start | bytes 6148
  263.4 43.6 %copy-start.39 = (f32[1,1,512]{2,1,0:T(1,128)S(1)}, f32[1,1,512]{2,1,0:T(1,128)}, u32[]{:S(2)}) copy-start(f32[1,1,512]{2,1,0:T(1,128)} %get-tuple-element.176) | copy-start | bytes 6148
  263.4 43.6 %copy-start.40 = (f32[1,1,512]{2,1,0:T(1,128)S(1)}, f32[1,1,512]{2,1,0:T(1,128)}, u32[]{:S(2)}) copy-start(f32[1,1,512]{2,1,0:T(1,128)} %get-tuple-element.177) | copy-start | bytes 6148
  263.4 43.6 %copy-start.41 = (f32[1,1,512]{2,1,0:T(1,128)S(1)}, f32[1,1,512]{2,1,0:T(1,128)}, u32[]{:S(2)}) copy-start(f32[1,1,512]{2,1,0:T(1,128)} %get-tuple-element.178) | copy-start | bytes 6148
  263.4 43.6 %copy-start.42 = (f32[1,1,512]{2,1,0:T(1,128)S(1)}, f32[1,1,512]{2,1,0:T(1,128)}, u32[]{:S(2)}) copy-start(f32[1,1,512]{2,1,0:T(1,128)} %get-tuple-element.179) | copy-start | bytes 6148
  263.4 43.6 %copy-start.43 = (f32[1,1,512]{2,1,0:T(1,128)S(1)}, f32[1,1,512]{2,1,0:T(1,128)}, u32[]{:S(2)}) copy-start(f32[1,1,512]{2,1,0:T(1,128)} %get-tuple-element.180) | copy-start | bytes 6148
  263.4 43.6 %copy-start.44 = (f32[1,1,512]{2,1,0:T(1,128)S(1)}, f32[1,1,512]{2,1,0:T(1,128)}, u32[]{:S(2)}) copy-start(f32[1,1,512]{2,1,0:T(1,128)} %get-tuple-element.181) | copy-start | bytes 6148
  264.7 31.3 %collective-permute-start = (bf16[3,64,512]{2,1,0:T(8,128)(2,1)S(1)}, bf16[3,64,512]{2,1,0:T(8,128)(2,1)S(1)}, u32[]{:S(2)}, u32[]{:S(2)}) collective-permute-start(bf16[3,64,512]{2,1,0:T(8,128)(2,1)S(1)} %bitcast.216), channel_id=1, source_target_pairs={{0,1},{1,2},{2,3},{3,4},{4,5},{5,6},{6,7},{7,8},{8,9},{9,10},{10,1... | collective-permute-start | bytes 589832 | tf_op jit(solution)/shard_map/ppermute | solution.py:24
  273.0 33.4 %collective-permute-start.1 = (bf16[3,64,512]{2,1,0:T(8,128)(2,1)S(1)}, bf16[3,64,512]{2,1,0:T(8,128)(2,1)S(1)}, u32[]{:S(2)}, u32[]{:S(2)}) collective-permute-start(bf16[3,64,512]{2,1,0:T(8,128)(2,1)S(1)} %bitcast.215), channel_id=1, source_target_pairs={{1,0},{2,1},{3,2},{4,3},{5,4},{6,5},{7,6},{8,7},{9,8},{10,9},{11,1... | collective-permute-start | bytes 589832 | tf_op jit(solution)/shard_map/ppermute | solution.py:27
  310.9 105.0 %copy-start.67 = (s32[4,1]{0,1:T(1,128)S(1)}, s32[4,1]{0,1:T(1,128)}, u32[]{:S(2)}) copy-start(s32[4,1]{0,1:T(1,128)} %param.43) | copy-start | bytes 52
  311.0 105.7 %copy-start.10 = (bf16[256,16]{0,1:T(8,128)(2,1)S(1)}, bf16[256,16]{0,1:T(8,128)(2,1)}, u32[]{:S(2)}) copy-start(bf16[256,16]{0,1:T(8,128)(2,1)} %param.42) | copy-start | bytes 24580
  402.5 136.3 %copy-start = (bf16[64,16,256]{2,1,0:T(8,128)(2,1)S(1)}, bf16[64,16,256]{2,1,0:T(8,128)(2,1)}, u32[]{:S(2)}) copy-start(bf16[64,16,256]{2,1,0:T(8,128)(2,1)} %param.34) | copy-start | bytes 1572868
  403.7 135.7 %copy-start.6 = (f32[7,7,256]{2,1,0:T(8,128)S(1)}, f32[7,7,256]{2,1,0:T(8,128)}, u32[]{:S(2)}) copy-start(f32[7,7,256]{2,1,0:T(8,128)} %param.40) | copy-start | bytes 150532
  403.7 137.4 %all-to-all-start = ((bf16[4,64,1024]{2,0,1:T(4,128)(2,1)}), bf16[4,64,1024]{2,0,1:T(4,128)(2,1)S(1)}, u32[]{:S(2)}, u32[]{:S(2)}) async-start(bf16[4,64,1024]{2,0,1:T(4,128)(2,1)} %copy.47), calls=%async_computation | async-start | bytes 1048576 | tf_op jit(solution)/shard_map/all_to_all | solution.py:151
  562.2 42.0 %copy-start.47 = (f32[1,1,256]{2,1,0:T(1,128)S(1)}, f32[1,1,256]{2,1,0:T(1,128)}, u32[]{:S(2)}) copy-start(f32[1,1,256]{2,1,0:T(1,128)} %get-tuple-element.218) | copy-start | bytes 3076
  562.2 42.0 %copy-start.48 = (f32[1,1,256]{2,1,0:T(1,128)S(1)}, f32[1,1,256]{2,1,0:T(1,128)}, u32[]{:S(2)}) copy-start(f32[1,1,256]{2,1,0:T(1,128)} %get-tuple-element.219) | copy-start | bytes 3076
  562.2 42.0 %copy-start.49 = (f32[1,1,256]{2,1,0:T(1,128)S(1)}, f32[1,1,256]{2,1,0:T(1,128)}, u32[]{:S(2)}) copy-start(f32[1,1,256]{2,1,0:T(1,128)} %get-tuple-element.220) | copy-start | bytes 3076
  562.2 42.0 %copy-start.50 = (f32[1,1,256]{2,1,0:T(1,128)S(1)}, f32[1,1,256]{2,1,0:T(1,128)}, u32[]{:S(2)}) copy-start(f32[1,1,256]{2,1,0:T(1,128)} %get-tuple-element.221) | copy-start | bytes 3076
  562.2 42.0 %copy-start.51 = (f32[1,1,256]{2,1,0:T(1,128)S(1)}, f32[1,1,256]{2,1,0:T(1,128)}, u32[]{:S(2)}) copy-start(f32[1,1,256]{2,1,0:T(1,128)} %get-tuple-element.222) | copy-start | bytes 3076
  562.2 42.0 %copy-start.52 = (f32[1,1,256]{2,1,0:T(1,128)S(1)}, f32[1,1,256]{2,1,0:T(1,128)}, u32[]{:S(2)}) copy-start(f32[1,1,256]{2,1,0:T(1,128)} %get-tuple-element.223) | copy-start | bytes 3076
  562.2 42.0 %copy-start.53 = (f32[1,1,256]{2,1,0:T(1,128)S(1)}, f32[1,1,256]{2,1,0:T(1,128)}, u32[]{:S(2)}) copy-start(f32[1,1,256]{2,1,0:T(1,128)} %get-tuple-element.224) | copy-start | bytes 3076
  562.2 42.0 %copy-start.54 = (f32[1,1,256]{2,1,0:T(1,128)S(1)}, f32[1,1,256]{2,1,0:T(1,128)}, u32[]{:S(2)}) copy-start(f32[1,1,256]{2,1,0:T(1,128)} %get-tuple-element.225) | copy-start | bytes 3076
  562.2 42.0 %copy-start.55 = (f32[1,1,256]{2,1,0:T(1,128)S(1)}, f32[1,1,256]{2,1,0:T(1,128)}, u32[]{:S(2)}) copy-start(f32[1,1,256]{2,1,0:T(1,128)} %get-tuple-element.226) | copy-start | bytes 3076
  562.3 42.0 %copy-start.56 = (f32[1,1,256]{2,1,0:T(1,128)S(1)}, f32[1,1,256]{2,1,0:T(1,128)}, u32[]{:S(2)}) copy-start(f32[1,1,256]{2,1,0:T(1,128)} %get-tuple-element.227) | copy-start | bytes 3076
  562.3 42.0 %copy-start.57 = (f32[1,1,256]{2,1,0:T(1,128)S(1)}, f32[1,1,256]{2,1,0:T(1,128)}, u32[]{:S(2)}) copy-start(f32[1,1,256]{2,1,0:T(1,128)} %get-tuple-element.228) | copy-start | bytes 3076
  562.3 42.0 %copy-start.58 = (f32[1,1,256]{2,1,0:T(1,128)S(1)}, f32[1,1,256]{2,1,0:T(1,128)}, u32[]{:S(2)}) copy-start(f32[1,1,256]{2,1,0:T(1,128)} %get-tuple-element.229) | copy-start | bytes 3076
  562.3 42.0 %copy-start.59 = (f32[1,1,256]{2,1,0:T(1,128)S(1)}, f32[1,1,256]{2,1,0:T(1,128)}, u32[]{:S(2)}) copy-start(f32[1,1,256]{2,1,0:T(1,128)} %get-tuple-element.230) | copy-start | bytes 3076
  563.1 8.3 %collective-permute-start.2 = (bf16[3,16,256]{2,1,0:T(8,128)(2,1)S(1)}, bf16[3,16,256]{2,1,0:T(8,128)(2,1)S(1)}, u32[]{:S(2)}, u32[]{:S(2)}) collective-permute-start(bf16[3,16,256]{2,1,0:T(8,128)(2,1)S(1)} %get-tuple-element.160), channel_id=1, source_target_pairs={{0,8},{8,16},{16,24},{24,32},{32,40},{40,48},{48,56},{56,64},{64,7... | collective-permute-start | bytes 73736 | tf_op jit(solution)/shard_map/ppermute | solution.py:24
  565.4 7.6 %collective-permute-start.3 = (bf16[3,16,256]{2,1,0:T(8,128)(2,1)S(1)}, bf16[3,16,256]{2,1,0:T(8,128)(2,1)S(1)}, u32[]{:S(2)}, u32[]{:S(2)}) collective-permute-start(bf16[3,16,256]{2,1,0:T(8,128)(2,1)S(1)} %get-tuple-element.159), channel_id=1, source_target_pairs={{8,0},{16,8},{24,16},{32,24},{40,32},{48,40},{56,48},{64,56},{72,6... | collective-permute-start | bytes 73736 | tf_op jit(solution)/shard_map/ppermute | solution.py:27
  574.1 15.7 %collective-permute-start.4 = (bf16[70,3,256]{2,1,0:T(4,128)(2,1)S(1)}, bf16[70,3,256]{2,1,0:T(4,128)(2,1)S(1)}, u32[]{:S(2)}, u32[]{:S(2)}) collective-permute-start(bf16[70,3,256]{2,1,0:T(4,128)(2,1)S(1)} %get-tuple-element.157), channel_id=1, source_target_pairs={{1,0},{2,1},{3,2},{4,3},{5,4},{6,5},{7,6},{9,8},{10,9},{11,10},{12... | collective-permute-start | bytes 322568 | tf_op jit(solution)/shard_map/ppermute | solution.py:27
  585.2 17.2 %collective-permute-start.5 = (bf16[70,3,256]{2,1,0:T(4,128)(2,1)S(1)}, bf16[70,3,256]{2,1,0:T(4,128)(2,1)S(1)}, u32[]{:S(2)}, u32[]{:S(2)}) collective-permute-start(bf16[70,3,256]{2,1,0:T(4,128)(2,1)S(1)} %get-tuple-element.158), channel_id=1, source_target_pairs={{0,1},{1,2},{2,3},{3,4},{4,5},{5,6},{6,7},{8,9},{9,10},{10,11},{11... | collective-permute-start | bytes 322568 | tf_op jit(solution)/shard_map/ppermute | solution.py:24
  (18 other events, 278.4 us)
Sparse Core Ops, SparseCore 0:
  9.5 127.7 all-gather.5
  139.5 118.6 all-gather.3
  260.4 140.4 all-gather.7
